TPU v7x, 32 devices: a whole 2x2x4 slice. The times are simulated.
32 devices in a mesh: groups: 2 (over y), freq: 4 (over x, core), recv: 4 (over z).
Axes of the slice: x: 2, y: 2, z: 4, core: 2. Of those that a mesh axis runs over, the one named last changes fastest.
Arguments:
- operator: bfloat16 [4, 32, 512, 2048], P('groups', 'freq', 'recv'), parts along dimension 0, may hold values from -0.125 to 0.125
- recorded: float32 [4, 32, 8, 512], P('groups', 'freq', None, 'recv'), parts along dimension 0, may hold values from -18 to 18
- win_start: int32 [16, 16], P('groups'), parts along dimension 0, may hold values from 0 to 15
- win_end: int32 [16, 16], P('groups'), parts along dimension 0, may hold values from 17 to 32
Outputs:
- reflectivity: float32 [4, 32, 8, 2048], P('groups', 'freq', None, 'recv'), parts along dimension 0
- residual: float32 [4, 32, 8, 512], P('groups', 'freq', None, 'recv'), parts along dimension 0
There are 2 independent parts, one for each index of `groups`. A program takes and returns all parts, laid end to end along the dimension named above; each array names one. Nothing has to cross between parts.
All inputs are finite; a program needn't handle non-finite values.
Results may differ from a plain program's by a relative error of at most 0.013.
Values may be sent and summed in bfloat16 or wider, within the bound.
No kernel may reach another device: no remote copies, remote signals or barrier semaphores. Data moves between devices by JAX's collectives and lax.ppermute only.
A program may use at most 64 MiB of HBM per device.

v0:
```python
import math
import jax
import jax.numpy as jnp
from jax import lax
from jax.sharding import PartitionSpec as P

SBLK = 128
ITERS = 5


def high_dot(left, right):
    return jnp.dot(left, right, precision=lax.Precision.HIGHEST)


def dft_rows(row_ids, length):
    positions = jnp.arange(length, dtype=jnp.int32)
    phases = (row_ids[:, None] * positions[None, :] % length).astype(jnp.float32) * (
        2.0 * math.pi / length
    )
    normalizer = 1.0 / math.sqrt(length)
    return (jnp.cos(phases) * normalizer, jnp.sin(phases) * normalizer)


def to_time(real_part, imag_part, cos_rows, sin_rows):
    time_real = high_dot(cos_rows.T, real_part) - high_dot(sin_rows.T, imag_part)
    time_imag = high_dot(sin_rows.T, real_part) + high_dot(cos_rows.T, imag_part)
    return (time_real, time_imag)


def to_freq(kept_real, kept_imag, cos_rows, sin_rows):
    real_part = high_dot(cos_rows, kept_real) + high_dot(sin_rows, kept_imag)
    imag_part = high_dot(cos_rows, kept_imag) - high_dot(sin_rows, kept_real)
    return jnp.stack([real_part, imag_part])


def window_mask(column_ids, src_local, win_start, win_end, length):
    blocks = win_start.shape[1]
    side_ids = column_ids // src_local
    source_ids = lax.axis_index("recv") * src_local + column_ids % src_local
    flat_ids = side_ids * blocks + source_ids // SBLK
    table_ids = jnp.arange(win_start.shape[0] * blocks, dtype=jnp.int32)
    matches = flat_ids[:, None] == table_ids[None, :]
    opening = jnp.sum(jnp.where(matches, win_start.reshape(-1)[None, :], 0), axis=1)
    closing = jnp.sum(jnp.where(matches, win_end.reshape(-1)[None, :], 0), axis=1)
    samples = jnp.arange(length, dtype=jnp.int32)[:, None]
    return ((samples >= opening[None, :]) & (samples < closing[None, :])).astype(jnp.float32)


def on_device(operator, recorded, win_start, win_end):
    freq_local = operator.shape[1]
    sources = operator.shape[3]
    right_sides = recorded.shape[2]
    src_local = sources // lax.axis_size("recv")
    total_freq = freq_local * lax.axis_size("freq")
    columns = right_sides * src_local
    real_operator = operator[0]
    imag_operator = operator[1]
    reflect = jnp.zeros((2, freq_local, right_sides, src_local), jnp.float32)
    residual = recorded
    for iteration in range(ITERS):
        rounded_residual = residual.astype(jnp.bfloat16)
        partial_real = jnp.einsum(
            "fbr,frs->fbs", rounded_residual[0], real_operator, preferred_element_type=jnp.float32
        ) + jnp.einsum(
            "fbr,frs->fbs", rounded_residual[1], imag_operator, preferred_element_type=jnp.float32
        )
        partial_imag = jnp.einsum(
            "fbr,frs->fbs", rounded_residual[1], real_operator, preferred_element_type=jnp.float32
        ) - jnp.einsum(
            "fbr,frs->fbs", rounded_residual[0], imag_operator, preferred_element_type=jnp.float32
        )
        gradient = lax.psum_scatter(
            jnp.stack([partial_real, partial_imag]).astype(jnp.bfloat16),
            "recv",
            scatter_dimension=3,
            tiled=True,
        ).astype(jnp.float32)
        flattened = gradient.reshape(2, freq_local, columns)
        empty_time = jnp.zeros((2, total_freq, columns), jnp.float32)
        segment = lax.all_gather(flattened.astype(jnp.bfloat16), "freq", axis=1, tiled=True).astype(
            jnp.float32
        )
        row_ids = jnp.arange(segment.shape[1], dtype=jnp.int32)
        cos_part, sin_part = dft_rows(row_ids, total_freq)
        part_real, part_imag = to_time(segment[0], segment[1], cos_part, sin_part)
        timed = empty_time + jnp.stack([part_real, part_imag])
        window = window_mask(
            jnp.arange(columns, dtype=jnp.int32), src_local, win_start, win_end, total_freq
        )
        own_rows = lax.axis_index("freq") * freq_local + jnp.arange(freq_local, dtype=jnp.int32)
        cos_rows, sin_rows = dft_rows(own_rows, total_freq)
        projected = to_freq(timed[0] * window, timed[1] * window, cos_rows, sin_rows)
        direction = projected.reshape(2, freq_local, right_sides, src_local)
        rounded_direction = direction.astype(jnp.bfloat16)
        add_segment = lax.all_gather(rounded_direction, "recv", axis=3, tiled=True)
        image_real = jnp.einsum(
            "fbs,frs->fbr", add_segment[0], real_operator, preferred_element_type=jnp.float32
        ) - jnp.einsum(
            "fbs,frs->fbr", add_segment[1], imag_operator, preferred_element_type=jnp.float32
        )
        image_imag = jnp.einsum(
            "fbs,frs->fbr", add_segment[0], imag_operator, preferred_element_type=jnp.float32
        ) + jnp.einsum(
            "fbs,frs->fbr", add_segment[1], real_operator, preferred_element_type=jnp.float32
        )
        image = jnp.stack([image_real, image_imag])
        direction_power, image_energy = lax.psum(
            (jnp.sum(direction * direction), jnp.sum(image * image)), ("freq", "recv")
        )
        step_length = direction_power / (image_energy + 1e-06)
        reflect = reflect + step_length * direction
        residual = residual - step_length * image
    return (reflect, residual)


def solution(mesh):
    return jax.shard_map(
        on_device,
        mesh=mesh,
        in_specs=(
            P("groups", "freq", "recv", None),
            P("groups", "freq", None, "recv"),
            P("groups", None),
            P("groups", None),
        ),
        out_specs=(P("groups", "freq", None, "recv"), P("groups", "freq", None, "recv")),
        check_vma=False,
    )
```

profile of v0, /device:TPU:0, one launch (start us, length us, event | category | flops | bytes accessed | tf_op | source)
XLA Modules:
  0.0 536.4 jit_solution(5900010467713200672)
XLA Ops:
  8.1 3.0 fusion.46
  11.0 3.3 fusion.48
  16.9 1.8 select_reduce_fusion.1
  18.7 22.4 %reduce-scatter.6.cloned.1.call-done = bf16[2,8,8,512]{3,2,1,0:T(8,128)(2,1)} async-done(((bf16[2,8,8,2048]{3,2,1,0:T(8,128)(2,1)}), bf16[2,8,8,512]{3,2,1,0:T(8,128)(2,1)}) %reduce-scatter.6.cloned.1.call-update) | async-done | bytes 131088 | tf_op jit(solution)/shard_map/reduce_scatter | solution.py:72
  41.1 1.0 convert_element_type.125
  42.1 7.1 %all_gather.30 = bf16[2,32,4096]{2,1,0:T(8,128)(2,1)S(1)} all-gather(bf16[2,8,4096]{2,1,0:T(8,128)(2,1)S(1)} %convert_element_type.125), channel_id=1, replica_groups=mesh['groups'=2,'freq'=4,'recv'=4] {'freq'}, dimensions={1}, use_global_device_ids=true | all-gather | bytes 655360 | tf_op jit(solution)/shard_map/all_gather | solution.py:80
  54.0 16.1 %all_gather.31 = bf16[2,8,8,2048]{3,2,1,0:T(8,128)(2,1)S(1)} all-gather(bf16[2,8,8,512]{3,2,1,0:T(8,128)(2,1)S(1)} %get-tuple-element.27), channel_id=1, replica_groups=mesh['groups'=2,'freq'=4,'recv'=4] {'recv'}, dimensions={3}, use_global_device_ids=true | all-gather | bytes 655360 | tf_op jit(solution)/shard_map/all_gather | solution.py:95
  70.1 3.5 fusion.42
  73.6 3.4 fusion.44
  77.1 1.2 fusion.189
  78.2 1.2 fusion.183
  80.1 30.5 %all-reduce.4 = (f32[]{:T(128)}, f32[]{:T(128)}) all-reduce(f32[]{:T(128)} %get-tuple-element.26, f32[]{:T(128)} %multiply_reduce_fusion.9), channel_id=1, replica_groups=mesh['groups'=2,'freq'=4,'recv'=4] {'freq','recv'}, use_global_device_ids=true, to_apply=%region_4.5 | all-reduce | flops 2 | bytes 16 | tf_op jit(solution)/shard_map/psum | solution.py:107
  111.9 2.8 fusion.38
  114.7 2.8 fusion.40
  117.6 2.9 fusion.159
  120.4 2.9 fusion.156
  124.2 21.0 %reduce-scatter.8.cloned.1.call-done = bf16[2,8,8,512]{3,2,1,0:T(8,128)(2,1)} async-done(((bf16[2,8,8,2048]{3,2,1,0:T(8,128)(2,1)}), bf16[2,8,8,512]{3,2,1,0:T(8,128)(2,1)}) %reduce-scatter.8.cloned.1.call-update) | async-done | bytes 131088 | tf_op jit(solution)/shard_map/reduce_scatter | solution.py:72
  145.2 1.0 convert_element_type.128
  146.2 7.1 %all_gather.32 = bf16[2,32,4096]{2,1,0:T(8,128)(2,1)S(1)} all-gather(bf16[2,8,4096]{2,1,0:T(8,128)(2,1)S(1)} %convert_element_type.128), channel_id=1, replica_groups=mesh['groups'=2,'freq'=4,'recv'=4] {'freq'}, dimensions={1}, use_global_device_ids=true | all-gather | bytes 655360 | tf_op jit(solution)/shard_map/all_gather | solution.py:80
  158.2 16.1 %all_gather.33 = bf16[2,8,8,2048]{3,2,1,0:T(8,128)(2,1)S(1)} all-gather(bf16[2,8,8,512]{3,2,1,0:T(8,128)(2,1)S(1)} %get-tuple-element.25), channel_id=1, replica_groups=mesh['groups'=2,'freq'=4,'recv'=4] {'recv'}, dimensions={3}, use_global_device_ids=true | all-gather | bytes 655360 | tf_op jit(solution)/shard_map/all_gather | solution.py:95
  174.2 3.5 fusion.34
  177.8 3.4 fusion.36
  181.1 1.2 fusion.201
  182.3 1.2 fusion.195
  184.2 30.5 %all-reduce.3 = (f32[]{:T(128)}, f32[]{:T(128)}) all-reduce(f32[]{:T(128)} %get-tuple-element.24, f32[]{:T(128)} %multiply_reduce_fusion.8), channel_id=1, replica_groups=mesh['groups'=2,'freq'=4,'recv'=4] {'freq','recv'}, use_global_device_ids=true, to_apply=%region_9.10 | all-reduce | flops 2 | bytes 16 | tf_op jit(solution)/shard_map/psum | solution.py:107
  216.0 2.8 fusion.30
  218.9 2.8 fusion.32
  221.7 2.9 fusion.165
  224.6 2.9 fusion.162
  228.4 21.0 %reduce-scatter.10.cloned.1.call-done = bf16[2,8,8,512]{3,2,1,0:T(8,128)(2,1)} async-done(((bf16[2,8,8,2048]{3,2,1,0:T(8,128)(2,1)}), bf16[2,8,8,512]{3,2,1,0:T(8,128)(2,1)}) %reduce-scatter.10.cloned.1.call-update) | async-done | bytes 131088 | tf_op jit(solution)/shard_map/reduce_scatter | solution.py:72
  249.3 1.0 convert_element_type.131
  250.3 7.1 %all_gather.34 = bf16[2,32,4096]{2,1,0:T(8,128)(2,1)S(1)} all-gather(bf16[2,8,4096]{2,1,0:T(8,128)(2,1)S(1)} %convert_element_type.131), channel_id=1, replica_groups=mesh['groups'=2,'freq'=4,'recv'=4] {'freq'}, dimensions={1}, use_global_device_ids=true | all-gather | bytes 655360 | tf_op jit(solution)/shard_map/all_gather | solution.py:80
  262.3 16.1 %all_gather.35 = bf16[2,8,8,2048]{3,2,1,0:T(8,128)(2,1)S(1)} all-gather(bf16[2,8,8,512]{3,2,1,0:T(8,128)(2,1)S(1)} %get-tuple-element.23), channel_id=1, replica_groups=mesh['groups'=2,'freq'=4,'recv'=4] {'recv'}, dimensions={3}, use_global_device_ids=true | all-gather | bytes 655360 | tf_op jit(solution)/shard_map/all_gather | solution.py:95
  278.4 3.5 fusion.26
  281.9 3.4 fusion.28
  285.3 1.2 fusion.213
  286.5 1.2 fusion.207
  288.3 30.7 %all-reduce.2 = (f32[]{:T(128)}, f32[]{:T(128)}) all-reduce(f32[]{:T(128)} %get-tuple-element.22, f32[]{:T(128)} %multiply_reduce_fusion.7), channel_id=1, replica_groups=mesh['groups'=2,'freq'=4,'recv'=4] {'freq','recv'}, use_global_device_ids=true, to_apply=%region_14.15 | all-reduce | flops 2 | bytes 16 | tf_op jit(solution)/shard_map/psum | solution.py:107
  320.3 2.8 fusion.22
  323.2 2.8 fusion.24
  326.0 2.9 fusion.171
  328.9 2.9 fusion.168
  332.7 20.9 %reduce-scatter.12.cloned.1.call-done = bf16[2,8,8,512]{3,2,1,0:T(8,128)(2,1)} async-done(((bf16[2,8,8,2048]{3,2,1,0:T(8,128)(2,1)}), bf16[2,8,8,512]{3,2,1,0:T(8,128)(2,1)}) %reduce-scatter.12.cloned.1.call-update) | async-done | bytes 131088 | tf_op jit(solution)/shard_map/reduce_scatter | solution.py:72
  353.6 1.0 convert_element_type.134
  354.5 7.2 %all_gather.36 = bf16[2,32,4096]{2,1,0:T(8,128)(2,1)S(1)} all-gather(bf16[2,8,4096]{2,1,0:T(8,128)(2,1)S(1)} %convert_element_type.134), channel_id=1, replica_groups=mesh['groups'=2,'freq'=4,'recv'=4] {'freq'}, dimensions={1}, use_global_device_ids=true | all-gather | bytes 655360 | tf_op jit(solution)/shard_map/all_gather | solution.py:80
  366.6 16.1 %all_gather.37 = bf16[2,8,8,2048]{3,2,1,0:T(8,128)(2,1)S(1)} all-gather(bf16[2,8,8,512]{3,2,1,0:T(8,128)(2,1)S(1)} %get-tuple-element.21), channel_id=1, replica_groups=mesh['groups'=2,'freq'=4,'recv'=4] {'recv'}, dimensions={3}, use_global_device_ids=true | all-gather | bytes 655360 | tf_op jit(solution)/shard_map/all_gather | solution.py:95
  382.7 3.5 fusion.18
  386.2 3.4 fusion.20
  389.6 1.2 fusion.225
  390.8 1.2 fusion.219
  392.6 30.5 %all-reduce.1 = (f32[]{:T(128)}, f32[]{:T(128)}) all-reduce(f32[]{:T(128)} %get-tuple-element.20, f32[]{:T(128)} %multiply_reduce_fusion.6), channel_id=1, replica_groups=mesh['groups'=2,'freq'=4,'recv'=4] {'freq','recv'}, use_global_device_ids=true, to_apply=%region_19.20 | all-reduce | flops 2 | bytes 16 | tf_op jit(solution)/shard_map/psum | solution.py:107
  424.4 2.8 fusion.14
  427.3 2.8 fusion.16
  430.1 2.9 fusion.177
  433.0 2.9 fusion.174
  436.7 20.9 %reduce-scatter.14.cloned.1.call-done = bf16[2,8,8,512]{3,2,1,0:T(8,128)(2,1)} async-done(((bf16[2,8,8,2048]{3,2,1,0:T(8,128)(2,1)}), bf16[2,8,8,512]{3,2,1,0:T(8,128)(2,1)}) %reduce-scatter.14.cloned.1.call-update) | async-done | bytes 131088 | tf_op jit(solution)/shard_map/reduce_scatter | solution.py:72
  457.6 1.0 convert_element_type.137
  458.6 7.1 %all_gather.38 = bf16[2,32,4096]{2,1,0:T(8,128)(2,1)S(1)} all-gather(bf16[2,8,4096]{2,1,0:T(8,128)(2,1)S(1)} %convert_element_type.137), channel_id=1, replica_groups=mesh['groups'=2,'freq'=4,'recv'=4] {'freq'}, dimensions={1}, use_global_device_ids=true | all-gather | bytes 655360 | tf_op jit(solution)/shard_map/all_gather | solution.py:80
  470.5 16.1 %all_gather.39 = bf16[2,8,8,2048]{3,2,1,0:T(8,128)(2,1)S(1)} all-gather(bf16[2,8,8,512]{3,2,1,0:T(8,128)(2,1)S(1)} %get-tuple-element.18), channel_id=1, replica_groups=mesh['groups'=2,'freq'=4,'recv'=4] {'recv'}, dimensions={3}, use_global_device_ids=true | all-gather | bytes 655360 | tf_op jit(solution)/shard_map/all_gather | solution.py:95
  486.6 3.5 fusion.10
  490.2 3.4 fusion.12
  493.6 1.2 fusion.237
  494.8 1.2 fusion.231
  496.6 30.3 %all-reduce = (f32[]{:T(128)}, f32[]{:T(128)}) all-reduce(f32[]{:T(128)} %get-tuple-element.19, f32[]{:T(128)} %multiply_reduce_fusion.5), channel_id=1, replica_groups=mesh['groups'=2,'freq'=4,'recv'=4] {'freq','recv'}, use_global_device_ids=true, to_apply=%region_24.25 | all-reduce | flops 2 | bytes 16 | tf_op jit(solution)/shard_map/psum | solution.py:107
  (121 shorter events, 35.6 us)
Async XLA Ops:
  7.2 34.0 %reduce-scatter.6.cloned.1.call-start = ((), (), s32[]{:S(2)}) async-start(), calls=%async_computation.5 | async-start | bytes 655360 | tf_op jit(solution)/shard_map/reduce_scatter | solution.py:72
  8.1 6.3 %copy-start = (bf16[2,8,128,2048]{3,2,1,0:T(8,128)(2,1)S(1)}, bf16[2,8,128,2048]{3,2,1,0:T(8,128)(2,1)}, u32[]{:S(2)}) copy-start(bf16[2,8,128,2048]{3,2,1,0:T(8,128)(2,1)} %param.4) | copy-start | bytes 25165828
  15.1 1.6 copy-start.2
  15.1 1.7 copy-start.3
  16.6 128.6 %reduce-scatter.8.cloned.1.call-start = ((), (), s32[]{:S(2)}) async-start(), calls=%async_computation.6 | async-start | bytes 655360 | tf_op jit(solution)/shard_map/reduce_scatter | solution.py:72
  50.2 26.9 %slice-start = ((s8[8388608]{0:T(1024)(128)(4,1)}), s8[4194304]{0:T(1024)(128)(4,1)S(1)}, s32[]{:S(2)}) async-start(s8[8388608]{0:T(1024)(128)(4,1)} %bitcast.406), calls=%async_computation.10 | async-start | bytes 8388608
  70.1 6.9 %slice-start.1 = ((s8[8388608]{0:T(1024)(128)(4,1)}), s8[4194304]{0:T(1024)(128)(4,1)S(1)}, s32[]{:S(2)}) async-start(s8[8388608]{0:T(1024)(128)(4,1)} %bitcast.406), calls=%async_computation.11 | async-start | bytes 8388608
  77.0 34.8 %copy-start.1 = (f32[2,8,8,128]{3,2,1,0:T(8,128)S(1)}, f32[2,8,8,128]{3,2,1,0:T(8,128)}, u32[]{:S(2)}) copy-start(f32[2,8,8,128]{3,2,1,0:T(8,128)} %param.5) | copy-start | bytes 196612
  124.2 125.2 %reduce-scatter.10.cloned.1.call-start = ((), (), s32[]{:S(2)}) async-start(), calls=%async_computation.7 | async-start | bytes 655360 | tf_op jit(solution)/shard_map/reduce_scatter | solution.py:72
  154.3 26.9 %slice-start.2 = ((s8[8388608]{0:T(1024)(128)(4,1)}), s8[4194304]{0:T(1024)(128)(4,1)S(1)}, s32[]{:S(2)}) async-start(s8[8388608]{0:T(1024)(128)(4,1)} %bitcast.408), calls=%async_computation.12 | async-start | bytes 8388608
  174.2 6.9 %slice-start.3 = ((s8[8388608]{0:T(1024)(128)(4,1)}), s8[4194304]{0:T(1024)(128)(4,1)S(1)}, s32[]{:S(2)}) async-start(s8[8388608]{0:T(1024)(128)(4,1)} %bitcast.408), calls=%async_computation.13 | async-start | bytes 8388608
  228.3 125.3 %reduce-scatter.12.cloned.1.call-start = ((), (), s32[]{:S(2)}) async-start(), calls=%async_computation.8 | async-start | bytes 655360 | tf_op jit(solution)/shard_map/reduce_scatter | solution.py:72
  257.9 27.3 %slice-start.4 = ((s8[8388608]{0:T(1024)(128)(4,1)}), s8[4194304]{0:T(1024)(128)(4,1)S(1)}, s32[]{:S(2)}) async-start(s8[8388608]{0:T(1024)(128)(4,1)} %bitcast.410), calls=%async_computation.14 | async-start | bytes 8388608
  278.4 6.9 %slice-start.5 = ((s8[8388608]{0:T(1024)(128)(4,1)}), s8[4194304]{0:T(1024)(128)(4,1)S(1)}, s32[]{:S(2)}) async-start(s8[8388608]{0:T(1024)(128)(4,1)} %bitcast.410), calls=%async_computation.15 | async-start | bytes 8388608
  332.6 125.0 %reduce-scatter.14.cloned.1.call-start = ((), (), s32[]{:S(2)}) async-start(), calls=%async_computation.9 | async-start | bytes 655360 | tf_op jit(solution)/shard_map/reduce_scatter | solution.py:72
  362.7 26.9 %slice-start.6 = ((s8[8388608]{0:T(1024)(128)(4,1)}), s8[4194304]{0:T(1024)(128)(4,1)S(1)}, s32[]{:S(2)}) async-start(s8[8388608]{0:T(1024)(128)(4,1)} %bitcast.412), calls=%async_computation.16 | async-start | bytes 8388608
  382.7 6.9 %slice-start.7 = ((s8[8388608]{0:T(1024)(128)(4,1)}), s8[4194304]{0:T(1024)(128)(4,1)S(1)}, s32[]{:S(2)}) async-start(s8[8388608]{0:T(1024)(128)(4,1)} %bitcast.412), calls=%async_computation.17 | async-start | bytes 8388608
  465.7 27.9 %slice-start.8 = ((s8[8388608]{0:T(1024)(128)(4,1)}), s8[4194304]{0:T(1024)(128)(4,1)S(1)}, s32[]{:S(2)}) async-start(s8[8388608]{0:T(1024)(128)(4,1)} %bitcast.414), calls=%async_computation.18 | async-start | bytes 8388608
  486.6 6.9 %slice-start.9 = ((s8[8388608]{0:T(1024)(128)(4,1)}), s8[4194304]{0:T(1024)(128)(4,1)S(1)}, s32[]{:S(2)}) async-start(s8[8388608]{0:T(1024)(128)(4,1)} %bitcast.414), calls=%async_computation.19 | async-start | bytes 8388608
Sparse Core Ops, SparseCore 0:
  16.7 24.3 reduce-scatter.5
  124.3 20.9 reduce-scatter.7
  228.4 20.8 reduce-scatter.9
  332.7 20.7 reduce-scatter.11
  436.8 20.7 reduce-scatter.13
where the time goes:
time: 545 us; the launch traced here: 536 us
  blocking collectives  268 us (49%)
  matrix products  120 us (22%)
  waiting for transfers between devices  106 us (19%)
  between operations  21 us (4%)
  other arithmetic  15 us (3%)
  local copies, waits for them, and re-layouts  5.9 us (1%)
    psum x5, blocking collectives, on_device(): lax.psum((jnp.sum(direction * direction), jnp.sum(image * image)), ('freq...  152 us
    reduce_scatter x5, waiting for transfers between devices, on_device(): lax.psum_scatter(jnp.stack([partial_real, partial_imag]).astype(jnp.bfloa...  106 us
    all_gather x5, blocking collectives, on_device(): add_segment = lax.all_gather(rounded_direction, 'recv', axis=3, tiled=True)  80.4 us
    all_gather x5, blocking collectives, on_device(): lax.all_gather(flattened.astype(jnp.bfloat16), 'freq', axis=1, tiled=True)  35.6 us
    dot_general x40, matrix products, high_dot(): return jnp.dot(left, right, precision=lax.Precision.HIGHEST)  19.8 us
    dot_general x5, matrix products, on_device(): jnp.einsum('fbs,frs->fbr', add_segment[0], imag_operator, preferred_eleme...  17.6 us
    dot_general x5, matrix products, on_device(): jnp.einsum('fbs,frs->fbr', add_segment[1], imag_operator, preferred_eleme...  16.9 us
    dot_general x5, matrix products, on_device(): jnp.einsum('fbr,frs->fbs', rounded_residual[1], imag_operator, preferred_...  14.7 us
  transfers between devices with their start and end apart: 5, of which 5 were waited for; matrix products, arithmetic and copies ran while one was open for 0% of the time, Pallas kernels for 0%

commit v1 on v0

--- a/solution.py
+++ b/solution.py
@@ -105,7 +105,7 @@
         )
         image = jnp.stack([image_real, image_imag])
         direction_power, image_energy = lax.psum(
-            (jnp.sum(direction * direction), jnp.sum(image * image)), ("freq", "recv")
+            lax.psum((jnp.sum(direction * direction), jnp.sum(image * image)), "recv"), "freq"
         )
         step_length = direction_power / (image_energy + 1e-06)
         reflect = reflect + step_length * direction

time: 545 us -> 470 us (0.86)
  blocking collectives: 268 us -> 195 us
    psum x5 -> x10, blocking collectives: 152 us -> 79.4 us  [the longest x5 47.1 us: on_device(): lax.psum((jnp.sum(direction * direction), jnp.sum(image * image)), 'recv')]
where the time goes in v1:
time: 470 us; the launch traced here: 461 us
  blocking collectives  195 us (41%)
  matrix products  120 us (26%)
  waiting for transfers between devices  104 us (22%)
  between operations  21 us (4%)
  other arithmetic  15 us (3%)
  local copies, waits for them, and re-layouts  5.9 us (1%)
    reduce_scatter x5, waiting for transfers between devices, on_device(): lax.psum_scatter(jnp.stack([partial_real, partial_imag]).astype(jnp.bfloa...  104 us
    all_gather x5, blocking collectives, on_device(): add_segment = lax.all_gather(rounded_direction, 'recv', axis=3, tiled=True)  80.4 us
    psum x5, blocking collectives, on_device(): lax.psum((jnp.sum(direction * direction), jnp.sum(image * image)), 'recv')  47.1 us
    all_gather x5, blocking collectives, on_device(): lax.all_gather(flattened.astype(jnp.bfloat16), 'freq', axis=1, tiled=True)  35.3 us
    psum x5, blocking collectives, on_device(): lax.psum(lax.psum((jnp.sum(direction * direction), jnp.sum(image * image)...  32.3 us
    dot_general x40, matrix products, high_dot(): return jnp.dot(left, right, precision=lax.Precision.HIGHEST)  19.8 us
    dot_general x5, matrix products, on_device(): jnp.einsum('fbs,frs->fbr', add_segment[0], imag_operator, preferred_eleme...  17.6 us
    dot_general x5, matrix products, on_device(): jnp.einsum('fbs,frs->fbr', add_segment[1], imag_operator, preferred_eleme...  16.9 us
  transfers between devices with their start and end apart: 5, of which 5 were waited for; matrix products, arithmetic and copies ran while one was open for 0% of the time, Pallas kernels for 0%

profile of v1, /device:TPU:0, one launch (start us, length us, event | category | flops | bytes accessed | tf_op | source)
XLA Modules:
  0.0 460.6 jit_solution(11742091682390537614)
XLA Ops:
  8.1 3.0 fusion.46
  11.0 3.3 fusion.48
  16.9 1.8 select_reduce_fusion.1
  18.7 22.4 %reduce-scatter.6.cloned.1.call-done = bf16[2,8,8,512]{3,2,1,0:T(8,128)(2,1)} async-done(((bf16[2,8,8,2048]{3,2,1,0:T(8,128)(2,1)}), bf16[2,8,8,512]{3,2,1,0:T(8,128)(2,1)}) %reduce-scatter.6.cloned.1.call-update) | async-done | bytes 131088 | tf_op jit(solution)/shard_map/reduce_scatter | solution.py:72
  42.1 7.1 %all_gather.30 = bf16[2,32,4096]{2,1,0:T(8,128)(2,1)S(1)} all-gather(bf16[2,8,4096]{2,1,0:T(8,128)(2,1)S(1)} %convert_element_type.125), channel_id=1, replica_groups=mesh['groups'=2,'freq'=4,'recv'=4] {'freq'}, dimensions={1}, use_global_device_ids=true | all-gather | bytes 655360 | tf_op jit(solution)/shard_map/all_gather | solution.py:80
  54.0 16.1 %all_gather.31 = bf16[2,8,8,2048]{3,2,1,0:T(8,128)(2,1)S(1)} all-gather(bf16[2,8,8,512]{3,2,1,0:T(8,128)(2,1)S(1)} %get-tuple-element.37), channel_id=1, replica_groups=mesh['groups'=2,'freq'=4,'recv'=4] {'recv'}, dimensions={3}, use_global_device_ids=true | all-gather | bytes 655360 | tf_op jit(solution)/shard_map/all_gather | solution.py:95
  70.1 3.5 fusion.42
  73.6 3.4 fusion.44
  77.1 1.2 fusion.189
  78.2 1.2 fusion.183
  80.1 9.4 %all-reduce.4 = (f32[]{:T(128)}, f32[]{:T(128)}) all-reduce(f32[]{:T(128)} %get-tuple-element.36, f32[]{:T(128)} %multiply_reduce_fusion.9), channel_id=1, replica_groups=mesh['groups'=2,'freq'=4,'recv'=4] {'recv'}, use_global_device_ids=true, to_apply=%region_4.5 | all-reduce | flops 2 | bytes 16 | tf_op jit(solution)/shard_map/psum | solution.py:108
  89.5 6.4 %all-reduce.9 = (f32[]{:T(128)}, f32[]{:T(128)}) all-reduce(f32[]{:T(128)} %get-tuple-element.12, f32[]{:T(128)} %get-tuple-element.13), channel_id=1, replica_groups=mesh['groups'=2,'freq'=4,'recv'=4] {'freq'}, use_global_device_ids=true, to_apply=%region_5.6 | all-reduce | flops 2 | bytes 16 | tf_op jit(solution)/shard_map/psum | solution.py:107
  97.3 2.8 fusion.38
  100.1 2.8 fusion.40
  103.0 2.9 fusion.159
  105.8 2.9 fusion.156
  109.6 20.4 %reduce-scatter.8.cloned.1.call-done = bf16[2,8,8,512]{3,2,1,0:T(8,128)(2,1)} async-done(((bf16[2,8,8,2048]{3,2,1,0:T(8,128)(2,1)}), bf16[2,8,8,512]{3,2,1,0:T(8,128)(2,1)}) %reduce-scatter.8.cloned.1.call-update) | async-done | bytes 131088 | tf_op jit(solution)/shard_map/reduce_scatter | solution.py:72
  130.9 7.1 %all_gather.32 = bf16[2,32,4096]{2,1,0:T(8,128)(2,1)S(1)} all-gather(bf16[2,8,4096]{2,1,0:T(8,128)(2,1)S(1)} %convert_element_type.128), channel_id=1, replica_groups=mesh['groups'=2,'freq'=4,'recv'=4] {'freq'}, dimensions={1}, use_global_device_ids=true | all-gather | bytes 655360 | tf_op jit(solution)/shard_map/all_gather | solution.py:80
  142.9 16.1 %all_gather.33 = bf16[2,8,8,2048]{3,2,1,0:T(8,128)(2,1)S(1)} all-gather(bf16[2,8,8,512]{3,2,1,0:T(8,128)(2,1)S(1)} %get-tuple-element.35), channel_id=1, replica_groups=mesh['groups'=2,'freq'=4,'recv'=4] {'recv'}, dimensions={3}, use_global_device_ids=true | all-gather | bytes 655360 | tf_op jit(solution)/shard_map/all_gather | solution.py:95
  159.0 3.5 fusion.34
  162.5 3.4 fusion.36
  165.9 1.2 fusion.201
  167.1 1.2 fusion.195
  168.9 9.4 %all-reduce.3 = (f32[]{:T(128)}, f32[]{:T(128)}) all-reduce(f32[]{:T(128)} %get-tuple-element.34, f32[]{:T(128)} %multiply_reduce_fusion.8), channel_id=1, replica_groups=mesh['groups'=2,'freq'=4,'recv'=4] {'recv'}, use_global_device_ids=true, to_apply=%region_11.12 | all-reduce | flops 2 | bytes 16 | tf_op jit(solution)/shard_map/psum | solution.py:108
  178.3 6.5 %all-reduce.8 = (f32[]{:T(128)}, f32[]{:T(128)}) all-reduce(f32[]{:T(128)} %get-tuple-element.10, f32[]{:T(128)} %get-tuple-element.11), channel_id=1, replica_groups=mesh['groups'=2,'freq'=4,'recv'=4] {'freq'}, use_global_device_ids=true, to_apply=%region_12.13 | all-reduce | flops 2 | bytes 16 | tf_op jit(solution)/shard_map/psum | solution.py:107
  186.2 2.8 fusion.30
  189.0 2.8 fusion.32
  191.8 2.9 fusion.165
  194.7 2.9 fusion.162
  198.5 20.3 %reduce-scatter.10.cloned.1.call-done = bf16[2,8,8,512]{3,2,1,0:T(8,128)(2,1)} async-done(((bf16[2,8,8,2048]{3,2,1,0:T(8,128)(2,1)}), bf16[2,8,8,512]{3,2,1,0:T(8,128)(2,1)}) %reduce-scatter.10.cloned.1.call-update) | async-done | bytes 131088 | tf_op jit(solution)/shard_map/reduce_scatter | solution.py:72
  219.7 7.1 %all_gather.34 = bf16[2,32,4096]{2,1,0:T(8,128)(2,1)S(1)} all-gather(bf16[2,8,4096]{2,1,0:T(8,128)(2,1)S(1)} %convert_element_type.131), channel_id=1, replica_groups=mesh['groups'=2,'freq'=4,'recv'=4] {'freq'}, dimensions={1}, use_global_device_ids=true | all-gather | bytes 655360 | tf_op jit(solution)/shard_map/all_gather | solution.py:80
  231.7 16.1 %all_gather.35 = bf16[2,8,8,2048]{3,2,1,0:T(8,128)(2,1)S(1)} all-gather(bf16[2,8,8,512]{3,2,1,0:T(8,128)(2,1)S(1)} %get-tuple-element.33), channel_id=1, replica_groups=mesh['groups'=2,'freq'=4,'recv'=4] {'recv'}, dimensions={3}, use_global_device_ids=true | all-gather | bytes 655360 | tf_op jit(solution)/shard_map/all_gather | solution.py:95
  247.8 3.5 fusion.26
  251.3 3.4 fusion.28
  254.7 1.2 fusion.213
  255.9 1.2 fusion.207
  257.7 9.4 %all-reduce.2 = (f32[]{:T(128)}, f32[]{:T(128)}) all-reduce(f32[]{:T(128)} %get-tuple-element.32, f32[]{:T(128)} %multiply_reduce_fusion.7), channel_id=1, replica_groups=mesh['groups'=2,'freq'=4,'recv'=4] {'recv'}, use_global_device_ids=true, to_apply=%region_18.19 | all-reduce | flops 2 | bytes 16 | tf_op jit(solution)/shard_map/psum | solution.py:108
  267.2 6.7 %all-reduce.7 = (f32[]{:T(128)}, f32[]{:T(128)}) all-reduce(f32[]{:T(128)} %get-tuple-element.8, f32[]{:T(128)} %get-tuple-element.9), channel_id=1, replica_groups=mesh['groups'=2,'freq'=4,'recv'=4] {'freq'}, use_global_device_ids=true, to_apply=%region_19.20 | all-reduce | flops 2 | bytes 16 | tf_op jit(solution)/shard_map/psum | solution.py:107
  275.2 2.8 fusion.22
  278.0 2.8 fusion.24
  280.9 2.9 fusion.171
  283.7 2.9 fusion.168
  287.5 20.2 %reduce-scatter.12.cloned.1.call-done = bf16[2,8,8,512]{3,2,1,0:T(8,128)(2,1)} async-done(((bf16[2,8,8,2048]{3,2,1,0:T(8,128)(2,1)}), bf16[2,8,8,512]{3,2,1,0:T(8,128)(2,1)}) %reduce-scatter.12.cloned.1.call-update) | async-done | bytes 131088 | tf_op jit(solution)/shard_map/reduce_scatter | solution.py:72
  308.7 6.9 %all_gather.36 = bf16[2,32,4096]{2,1,0:T(8,128)(2,1)S(1)} all-gather(bf16[2,8,4096]{2,1,0:T(8,128)(2,1)S(1)} %convert_element_type.134), channel_id=1, replica_groups=mesh['groups'=2,'freq'=4,'recv'=4] {'freq'}, dimensions={1}, use_global_device_ids=true | all-gather | bytes 655360 | tf_op jit(solution)/shard_map/all_gather | solution.py:80
  320.5 16.1 %all_gather.37 = bf16[2,8,8,2048]{3,2,1,0:T(8,128)(2,1)S(1)} all-gather(bf16[2,8,8,512]{3,2,1,0:T(8,128)(2,1)S(1)} %get-tuple-element.31), channel_id=1, replica_groups=mesh['groups'=2,'freq'=4,'recv'=4] {'recv'}, dimensions={3}, use_global_device_ids=true | all-gather | bytes 655360 | tf_op jit(solution)/shard_map/all_gather | solution.py:95
  336.6 3.5 fusion.18
  340.2 3.4 fusion.20
  343.5 1.2 fusion.225
  344.7 1.2 fusion.219
  346.6 9.4 %all-reduce.1 = (f32[]{:T(128)}, f32[]{:T(128)}) all-reduce(f32[]{:T(128)} %get-tuple-element.30, f32[]{:T(128)} %multiply_reduce_fusion.6), channel_id=1, replica_groups=mesh['groups'=2,'freq'=4,'recv'=4] {'recv'}, use_global_device_ids=true, to_apply=%region_25.26 | all-reduce | flops 2 | bytes 16 | tf_op jit(solution)/shard_map/psum | solution.py:108
  356.0 6.4 %all-reduce.6 = (f32[]{:T(128)}, f32[]{:T(128)}) all-reduce(f32[]{:T(128)} %get-tuple-element.6, f32[]{:T(128)} %get-tuple-element.7), channel_id=1, replica_groups=mesh['groups'=2,'freq'=4,'recv'=4] {'freq'}, use_global_device_ids=true, to_apply=%region_26.27 | all-reduce | flops 2 | bytes 16 | tf_op jit(solution)/shard_map/psum | solution.py:107
  363.8 2.8 fusion.14
  366.6 2.8 fusion.16
  369.5 2.9 fusion.177
  372.3 2.9 fusion.174
  376.1 20.4 %reduce-scatter.14.cloned.1.call-done = bf16[2,8,8,512]{3,2,1,0:T(8,128)(2,1)} async-done(((bf16[2,8,8,2048]{3,2,1,0:T(8,128)(2,1)}), bf16[2,8,8,512]{3,2,1,0:T(8,128)(2,1)}) %reduce-scatter.14.cloned.1.call-update) | async-done | bytes 131088 | tf_op jit(solution)/shard_map/reduce_scatter | solution.py:72
  397.4 7.1 %all_gather.38 = bf16[2,32,4096]{2,1,0:T(8,128)(2,1)S(1)} all-gather(bf16[2,8,4096]{2,1,0:T(8,128)(2,1)S(1)} %convert_element_type.137), channel_id=1, replica_groups=mesh['groups'=2,'freq'=4,'recv'=4] {'freq'}, dimensions={1}, use_global_device_ids=true | all-gather | bytes 655360 | tf_op jit(solution)/shard_map/all_gather | solution.py:80
  409.4 16.1 %all_gather.39 = bf16[2,8,8,2048]{3,2,1,0:T(8,128)(2,1)S(1)} all-gather(bf16[2,8,8,512]{3,2,1,0:T(8,128)(2,1)S(1)} %get-tuple-element.28), channel_id=1, replica_groups=mesh['groups'=2,'freq'=4,'recv'=4] {'recv'}, dimensions={3}, use_global_device_ids=true | all-gather | bytes 655360 | tf_op jit(solution)/shard_map/all_gather | solution.py:95
  425.5 3.5 fusion.10
  429.0 3.4 fusion.12
  432.4 1.2 fusion.237
  433.6 1.2 fusion.231
  435.4 9.4 %all-reduce = (f32[]{:T(128)}, f32[]{:T(128)}) all-reduce(f32[]{:T(128)} %get-tuple-element.29, f32[]{:T(128)} %multiply_reduce_fusion.5), channel_id=1, replica_groups=mesh['groups'=2,'freq'=4,'recv'=4] {'recv'}, use_global_device_ids=true, to_apply=%region_32.33 | all-reduce | flops 2 | bytes 16 | tf_op jit(solution)/shard_map/psum | solution.py:108
  444.8 6.3 %all-reduce.5 = (f32[]{:T(128)}, f32[]{:T(128)}) all-reduce(f32[]{:T(128)} %get-tuple-element.4, f32[]{:T(128)} %get-tuple-element.5), channel_id=1, replica_groups=mesh['groups'=2,'freq'=4,'recv'=4] {'freq'}, use_global_device_ids=true, to_apply=%region_33.34 | all-reduce | flops 2 | bytes 16 | tf_op jit(solution)/shard_map/psum | solution.py:107
  (126 shorter events, 40.5 us)
Async XLA Ops:
  7.2 34.0 %reduce-scatter.6.cloned.1.call-start = ((), (), s32[]{:S(2)}) async-start(), calls=%async_computation.5 | async-start | bytes 655360 | tf_op jit(solution)/shard_map/reduce_scatter | solution.py:72
  8.1 6.3 %copy-start = (bf16[2,8,128,2048]{3,2,1,0:T(8,128)(2,1)S(1)}, bf16[2,8,128,2048]{3,2,1,0:T(8,128)(2,1)}, u32[]{:S(2)}) copy-start(bf16[2,8,128,2048]{3,2,1,0:T(8,128)(2,1)} %param.4) | copy-start | bytes 25165828
  15.1 1.6 copy-start.2
  15.1 1.7 copy-start.3
  16.6 113.3 %reduce-scatter.8.cloned.1.call-start = ((), (), s32[]{:S(2)}) async-start(), calls=%async_computation.6 | async-start | bytes 655360 | tf_op jit(solution)/shard_map/reduce_scatter | solution.py:72
  50.2 26.9 %slice-start = ((s8[8388608]{0:T(1024)(128)(4,1)}), s8[4194304]{0:T(1024)(128)(4,1)S(1)}, s32[]{:S(2)}) async-start(s8[8388608]{0:T(1024)(128)(4,1)} %bitcast.406), calls=%async_computation.10 | async-start | bytes 8388608
  70.1 6.9 %slice-start.1 = ((s8[8388608]{0:T(1024)(128)(4,1)}), s8[4194304]{0:T(1024)(128)(4,1)S(1)}, s32[]{:S(2)}) async-start(s8[8388608]{0:T(1024)(128)(4,1)} %bitcast.406), calls=%async_computation.11 | async-start | bytes 8388608
  77.0 20.2 %copy-start.1 = (f32[2,8,8,128]{3,2,1,0:T(8,128)S(1)}, f32[2,8,8,128]{3,2,1,0:T(8,128)}, u32[]{:S(2)}) copy-start(f32[2,8,8,128]{3,2,1,0:T(8,128)} %param.5) | copy-start | bytes 196612
  109.6 109.2 %reduce-scatter.10.cloned.1.call-start = ((), (), s32[]{:S(2)}) async-start(), calls=%async_computation.7 | async-start | bytes 655360 | tf_op jit(solution)/shard_map/reduce_scatter | solution.py:72
  139.0 26.9 %slice-start.2 = ((s8[8388608]{0:T(1024)(128)(4,1)}), s8[4194304]{0:T(1024)(128)(4,1)S(1)}, s32[]{:S(2)}) async-start(s8[8388608]{0:T(1024)(128)(4,1)} %bitcast.408), calls=%async_computation.12 | async-start | bytes 8388608
  159.0 6.9 %slice-start.3 = ((s8[8388608]{0:T(1024)(128)(4,1)}), s8[4194304]{0:T(1024)(128)(4,1)S(1)}, s32[]{:S(2)}) async-start(s8[8388608]{0:T(1024)(128)(4,1)} %bitcast.408), calls=%async_computation.13 | async-start | bytes 8388608
  198.4 109.3 %reduce-scatter.12.cloned.1.call-start = ((), (), s32[]{:S(2)}) async-start(), calls=%async_computation.8 | async-start | bytes 655360 | tf_op jit(solution)/shard_map/reduce_scatter | solution.py:72
  227.3 27.4 %slice-start.4 = ((s8[8388608]{0:T(1024)(128)(4,1)}), s8[4194304]{0:T(1024)(128)(4,1)S(1)}, s32[]{:S(2)}) async-start(s8[8388608]{0:T(1024)(128)(4,1)} %bitcast.410), calls=%async_computation.14 | async-start | bytes 8388608
  247.8 6.9 %slice-start.5 = ((s8[8388608]{0:T(1024)(128)(4,1)}), s8[4194304]{0:T(1024)(128)(4,1)S(1)}, s32[]{:S(2)}) async-start(s8[8388608]{0:T(1024)(128)(4,1)} %bitcast.410), calls=%async_computation.15 | async-start | bytes 8388608
  287.5 109.0 %reduce-scatter.14.cloned.1.call-start = ((), (), s32[]{:S(2)}) async-start(), calls=%async_computation.9 | async-start | bytes 655360 | tf_op jit(solution)/shard_map/reduce_scatter | solution.py:72
  316.7 26.9 %slice-start.6 = ((s8[8388608]{0:T(1024)(128)(4,1)}), s8[4194304]{0:T(1024)(128)(4,1)S(1)}, s32[]{:S(2)}) async-start(s8[8388608]{0:T(1024)(128)(4,1)} %bitcast.412), calls=%async_computation.16 | async-start | bytes 8388608
  336.6 6.9 %slice-start.7 = ((s8[8388608]{0:T(1024)(128)(4,1)}), s8[4194304]{0:T(1024)(128)(4,1)S(1)}, s32[]{:S(2)}) async-start(s8[8388608]{0:T(1024)(128)(4,1)} %bitcast.412), calls=%async_computation.17 | async-start | bytes 8388608
  404.5 27.9 %slice-start.8 = ((s8[8388608]{0:T(1024)(128)(4,1)}), s8[4194304]{0:T(1024)(128)(4,1)S(1)}, s32[]{:S(2)}) async-start(s8[8388608]{0:T(1024)(128)(4,1)} %bitcast.414), calls=%async_computation.18 | async-start | bytes 8388608
  425.5 6.9 %slice-start.9 = ((s8[8388608]{0:T(1024)(128)(4,1)}), s8[4194304]{0:T(1024)(128)(4,1)S(1)}, s32[]{:S(2)}) async-start(s8[8388608]{0:T(1024)(128)(4,1)} %bitcast.414), calls=%async_computation.19 | async-start | bytes 8388608
Sparse Core Ops, SparseCore 0:
  16.7 24.3 reduce-scatter.5
  109.7 20.2 reduce-scatter.7
  198.6 20.1 reduce-scatter.9
  287.6 20.1 reduce-scatter.11
  376.2 20.2 reduce-scatter.13
